TPU v7x, 32 devices: a whole 2x2x4 slice. The times are simulated.
32 devices in a mesh: groups: 2 (over y), row: 4 (over x, core), col: 4 (over z).
Axes of the slice: x: 2, y: 2, z: 4, core: 2. Of those that a mesh axis runs over, the one named last changes fastest.
Arguments:
- tokens: float32 [256, 8192], P(('groups', 'row', 'col')), parts along dimension 0, may hold values from -36 to 36
- modulation: float32 [3, 2, 8192], P(None, 'groups'), parts along dimension 1, may hold values from -4 to 4
- up_weight: float32 [8192, 16384], P('row', 'col'), may hold values from -0.0625 to 0.0625
- up_bias: float32 [16384], P('col'), may hold values from -3 to 3
- down_weight: float32 [16384, 8192], P('col', 'row'), may hold values from -0.046875 to 0.046875
- down_bias: float32 [8192], replicated, may hold values from -3 to 3
Outputs:
- result: float32 [256, 8192], P(('groups', 'row', 'col')), parts along dimension 0
There are 2 independent parts, one for each index of `groups`. A program takes and returns all parts, laid end to end along the dimension named above; an argument that names none is the same for every part. Nothing has to cross between parts.
All inputs are finite; a program needn't handle non-finite values.
Results may differ from a plain program's by a relative error of at most 0.00005.
Values sent between devices are 32-bit elements; how exact they have to be, the bound alone decides.
No kernel may reach another device: no remote copies, remote signals or barrier semaphores. Data moves between devices by JAX's collectives and lax.ppermute only.
A program may use at most 128 MiB of HBM per device.

v0:
```python
import jax
import jax.numpy as jnp
from jax import lax
from jax.sharding import PartitionSpec as P

SEQ = 256
layer_eps = 1e-06


def local(tokens, modulation, up_weight, up_bias, down_weight, down_bias):
    tok_dev = tokens.shape[0]
    first_tok = (lax.axis_index("row") * lax.axis_size("col") + lax.axis_index("col")) * tok_dev
    sample = first_tok // SEQ
    own_mods = lax.dynamic_slice_in_dim(modulation, sample, 1, 1)[:, 0]
    shift_vec = own_mods[0]
    scale_vec = own_mods[1]
    gate_vec = own_mods[2]
    average = jnp.mean(tokens, axis=1, keepdims=True)
    centred = tokens - average
    spread_sq = jnp.mean(centred * centred, axis=1, keepdims=True)
    normed = centred * lax.rsqrt(spread_sq + layer_eps)
    mixed = normed * (1.0 + scale_vec) + shift_vec
    columns = lax.all_to_all(mixed, "row", split_axis=1, concat_axis=0, tiled=True)
    partial_value = jnp.dot(
        lax.all_gather(columns, "col", axis=0, tiled=True),
        up_weight,
        precision=lax.Precision.HIGH,
        preferred_element_type=jnp.float32,
    )
    own_share = lax.psum_scatter(partial_value, "row", scatter_dimension=0, tiled=True)
    activated_share = jax.nn.gelu(own_share + up_bias, approximate=True)
    activated = lax.all_gather(activated_share, "row", axis=0, tiled=True)
    out_share = lax.psum_scatter(
        jnp.dot(
            activated, down_weight, precision=lax.Precision.HIGH, preferred_element_type=jnp.float32
        ),
        "col",
        scatter_dimension=0,
        tiled=True,
    )
    returned = lax.all_to_all(out_share, "row", split_axis=0, concat_axis=1, tiled=True)
    return tokens + gate_vec * (returned + down_bias)


def solution(mesh):
    in_specs = (
        P(("groups", "row", "col"), None),
        P(None, "groups", None),
        P("row", "col"),
        P("col"),
        P("col", "row"),
        P(),
    )
    out_specs = P(("groups", "row", "col"), None)
    return jax.shard_map(local, mesh=mesh, in_specs=in_specs, out_specs=out_specs, check_vma=False)
```

profile of v0, /device:TPU:0, one launch (start us, length us, event | category | flops | bytes accessed | tf_op | source)
XLA Modules:
  0.0 183.2 jit_solution(12808481648443348210)
XLA Ops:
  6.5 0.0 copy-start.2
  6.5 0.0 all-gather.3.cloned.1.call-start
  6.5 1.1 reduce_sum.18
  7.7 1.2 multiply_reduce_fusion
  8.9 0.8 fusion.7
  9.7 1.1 multiply_add_fusion.1
  10.8 10.2 %all_to_all.38 = f32[8,4,2048]{2,0,1:T(8,128)} all-to-all(f32[8,4,2048]{2,0,1:T(8,128)S(1)} %bitcast.16), channel_id=1, replica_groups=mesh['groups'=2,'row'=4,'col'=4] {'row'}, dimensions={1} | all-to-all | bytes 524288 | tf_op jit(solution)/shard_map/all_to_all | solution.py:23
  20.9 0.0 all-gather.3.cloned.1.call-update
  21.0 0.0 copy-start
  21.0 0.0 copy-start.1
  21.0 0.0 reduce-scatter.3.cloned.1.call-start
  21.0 28.7 %all-gather.3.cloned.1.call-done = f32[128,2048]{1,0:T(8,128)} async-done(((f32[32,2048]{1,0:T(8,128)}), f32[128,2048]{1,0:T(8,128)}) %all-gather.3.cloned.1.call-update) | async-done | bytes 1048592 | tf_op jit(solution)/shard_map/all_gather | solution.py:25
  49.8 17.7 %fusion.8 = f32[128,4096]{1,0:T(8,128)} fusion(f32[128,2048]{1,0:T(8,128)} %all-gather.3.cloned.1.call-done, f32[2048,4096]{1,0:T(8,128)} %param.8), kind=kOutput, calls=%fused_computation.15 | convolution fusion | flops 6442450944 | bytes 36700160 | tf_op jit(solution)/shard_map/dot_general | solution.py:24
  67.5 0.0 reduce-scatter.3.cloned.1.call-update
  67.5 0.0 all-gather.5.cloned.1.call-start
  67.6 31.0 %reduce-scatter.3.cloned.1.call-done = f32[32,4096]{1,0:T(8,128)} async-done(((f32[128,4096]{1,0:T(8,128)}), f32[32,4096]{1,0:T(8,128)}) %reduce-scatter.3.cloned.1.call-update) | async-done | bytes 524304 | tf_op jit(solution)/shard_map/reduce_scatter | solution.py:30
  98.6 0.0 copy-done.2
  98.6 2.0 %fusion.6 = f32[32,4096]{1,0:T(8,128)} fusion(f32[32,4096]{1,0:T(8,128)} %reduce-scatter.3.cloned.1.call-done, f32[4096]{0:T(1024)S(1)} %copy-done.2), kind=kLoop, calls=%fused_computation.7 | loop fusion | flops 1179648 | bytes 1064960 | tf_op jit(solution)/shard_map/mul | solution.py:31
  100.6 0.0 all-gather.5.cloned.1.call-update
  100.7 0.0 reduce-scatter.5.cloned.1.call-start
  100.7 22.7 %all-gather.5.cloned.1.call-done = f32[128,4096]{1,0:T(8,128)} async-done(((f32[32,4096]{1,0:T(8,128)}), f32[128,4096]{1,0:T(8,128)}) %all-gather.5.cloned.1.call-update) | async-done | bytes 2097168 | tf_op jit(solution)/shard_map/all_gather | solution.py:32
  123.4 15.8 %fusion.9 = f32[128,2048]{1,0:T(8,128)} fusion(f32[128,4096]{1,0:T(8,128)} %all-gather.5.cloned.1.call-done, f32[4096,2048]{1,0:T(8,128)} %param.10), kind=kOutput, calls=%fused_computation.16 | convolution fusion | flops 6442450944 | bytes 36700160 | tf_op jit(solution)/shard_map/dot_general | solution.py:34
  139.2 0.0 reduce-scatter.5.cloned.1.call-update
  139.2 27.3 %reduce-scatter.5.cloned.1.call-done = f32[32,2048]{1,0:T(8,128)} async-done(((f32[128,2048]{1,0:T(8,128)}), f32[32,2048]{1,0:T(8,128)}) %reduce-scatter.5.cloned.1.call-update) | async-done | bytes 262160 | tf_op jit(solution)/shard_map/reduce_scatter | solution.py:33
  166.5 9.4 %all_to_all.39 = f32[4,8,2048]{2,1,0:T(8,128)S(1)} all-to-all(f32[4,8,2048]{2,1,0:T(8,128)} %bitcast.18), channel_id=1, replica_groups=mesh['groups'=2,'row'=4,'col'=4] {'row'}, dimensions={0} | all-to-all | bytes 524288 | tf_op jit(solution)/shard_map/all_to_all | solution.py:41
  175.9 0.0 copy-done
  175.9 0.0 copy-done.1
  175.9 0.8 multiply_add_fusion
  (2 shorter events, 0.0 us)
Async XLA Ops:
  6.5 92.1 %copy-start.2 = (f32[4096]{0:T(1024)S(1)}, f32[4096]{0:T(1024)}, u32[]{:S(2)}) copy-start(f32[4096]{0:T(1024)} %param.9) | copy-start | bytes 49156
  6.5 43.2 %all-gather.3.cloned.1.call-start = ((), (), s32[]{:S(2)}) async-start(), calls=%async_computation.4 | async-start | bytes 1310720 | tf_op jit(solution)/shard_map/all_gather | solution.py:25
  21.0 154.9 %copy-start = (f32[8,8192]{1,0:T(8,128)S(1)}, f32[8,8192]{1,0:T(8,128)}, u32[]{:S(2)}) copy-start(f32[8,8192]{1,0:T(8,128)} %param.6) | copy-start | bytes 786436
  21.0 154.9 %copy-start.1 = (f32[8192]{0:T(1024)S(1)}, f32[8192]{0:T(1024)}, u32[]{:S(2)}) copy-start(f32[8192]{0:T(1024)} %param.11) | copy-start | bytes 98308
  21.0 77.6 %reduce-scatter.3.cloned.1.call-start = ((), (), s32[]{:S(2)}) async-start(), calls=%async_computation.5 | async-start | bytes 2621440 | tf_op jit(solution)/shard_map/reduce_scatter | solution.py:30
  67.5 55.9 %all-gather.5.cloned.1.call-start = ((), (), s32[]{:S(2)}) async-start(), calls=%async_computation.6 | async-start | bytes 2621440 | tf_op jit(solution)/shard_map/all_gather | solution.py:32
  100.7 65.9 %reduce-scatter.5.cloned.1.call-start = ((), (), s32[]{:S(2)}) async-start(), calls=%async_computation.7 | async-start | bytes 1310720 | tf_op jit(solution)/shard_map/reduce_scatter | solution.py:33
Sparse Core Ops, SparseCore 0:
  21.1 28.6 all-gather.2
  67.6 30.9 reduce-scatter.2
  100.8 22.5 all-gather.4
  139.3 27.1 reduce-scatter.4
where the time goes:
time: 184 us; the launch traced here: 183 us
  waiting for transfers between devices  110 us (60%)
  matrix products  33.5 us (18%)
  blocking collectives  19.6 us (11%)
  between operations  13.2 us (7%)
  other arithmetic  7.04 us (4%)
    reduce_scatter x1, waiting for transfers between devices, local(): lax.psum_scatter(partial_value, 'row', scatter_dimension=0, tiled=True)  31 us
    all_gather x1, waiting for transfers between devices, local(): lax.all_gather(columns, 'col', axis=0, tiled=True)  28.7 us
    reduce_scatter x1, waiting for transfers between devices, local(): lax.psum_scatter(jnp.dot(activated, down_weight, precision=lax.Precision....  27.3 us
    all_gather x1, waiting for transfers between devices, local(): activated = lax.all_gather(activated_share, 'row', axis=0, tiled=True)  22.7 us
    dot_general x1, matrix products, local(): jnp.dot(lax.all_gather(columns, 'col', axis=0, tiled=True), up_weight, pr...  17.7 us
    dot_general x1, matrix products, local(): jnp.dot(activated, down_weight, precision=lax.Precision.HIGH, preferred_e...  15.8 us
    all_to_all x1, blocking collectives, local(): lax.all_to_all(mixed, 'row', split_axis=1, concat_axis=0, tiled=True)  10.2 us
    all_to_all x1, blocking collectives, local(): lax.all_to_all(out_share, 'row', split_axis=0, concat_axis=1, tiled=True)  9.41 us
  transfers between devices with their start and end apart: 4, of which 4 were waited for; matrix products, arithmetic and copies ran while one was open for 0% of the time, Pallas kernels for 0%

commit v1 on v0

--- a/solution.py
+++ b/solution.py
@@ -29,7 +29,12 @@
     )
     own_share = lax.psum_scatter(partial_value, "row", scatter_dimension=0, tiled=True)
     activated_share = jax.nn.gelu(own_share + up_bias, approximate=True)
-    activated = lax.all_gather(activated_share, "row", axis=0, tiled=True)
+    ring = [activated_share]
+    for hop in range(3):
+        ring.append(lax.ppermute(ring[-1], "row", [(dev, (dev + 1) % 4) for dev in range(4)]))
+    activated = jnp.roll(
+        jnp.concatenate(ring[::-1], axis=0), (lax.axis_index("row") + 1) * ring[0].shape[0], axis=0
+    )
     out_share = lax.psum_scatter(
         jnp.dot(
             activated, down_weight, precision=lax.Precision.HIGH, preferred_element_type=jnp.float32

time: 184 us -> 193 us (1.049)
  local copies, waits for them, and re-layouts: 0.02 us -> 4.99 us
  waiting for transfers between devices: 110 us -> 113 us
    ppermute x0 -> x3, waiting for transfers between devices: none -> 25.8 us  [local(): lax.ppermute(ring[-1], 'row', [(dev, (dev + 1) % 4) for dev in range(4)])]
    all_gather x1 -> x0, waiting for transfers between devices: 22.7 us -> none  [local(): activated = lax.all_gather(activated_share, 'row', axis=0, tiled=True)]
    unnamed x6 -> x14, local copies, waits for them, and re-layouts: 0.02 us -> 4.99 us
  transfers between devices with their start and end apart: 4 -> 6, of which waited for: 4 -> 6; matrix products, arithmetic and copies ran while one was open for 0% -> 0% of each run, Pallas kernels for 0% -> 0%
where the time goes in v1:
time: 193 us
  waiting for transfers between devices  113 us (59%)
  matrix products  33.5 us (17%)
  blocking collectives  19.6 us (10%)
  between operations  13.1 us (7%)
  other arithmetic  8.24 us (4%)
  local copies, waits for them, and re-layouts  4.99 us (3%)
    reduce_scatter x1, waiting for transfers between devices, local(): lax.psum_scatter(partial_value, 'row', scatter_dimension=0, tiled=True)  31 us
    all_gather x1, waiting for transfers between devices, local(): lax.all_gather(columns, 'col', axis=0, tiled=True)  28.7 us
    reduce_scatter x1, waiting for transfers between devices, local(): lax.psum_scatter(jnp.dot(activated, down_weight, precision=lax.Precision....  27.3 us
    ppermute x3, waiting for transfers between devices, local(): lax.ppermute(ring[-1], 'row', [(dev, (dev + 1) % 4) for dev in range(4)])  25.8 us
    dot_general x1, matrix products, local(): jnp.dot(lax.all_gather(columns, 'col', axis=0, tiled=True), up_weight, pr...  17.7 us
    dot_general x1, matrix products, local(): jnp.dot(activated, down_weight, precision=lax.Precision.HIGH, preferred_e...  15.8 us
    all_to_all x1, blocking collectives, local(): lax.all_to_all(mixed, 'row', split_axis=1, concat_axis=0, tiled=True)  10.2 us
    all_to_all x1, blocking collectives, local(): lax.all_to_all(out_share, 'row', split_axis=0, concat_axis=1, tiled=True)  9.41 us
  transfers between devices with their start and end apart: 6, of which 6 were waited for; matrix products, arithmetic and copies ran while one was open for 0% of the time, Pallas kernels for 0%

profile of v1, /device:TPU:0, one launch (start us, length us, event | category | flops | bytes accessed | tf_op | source)
XLA Modules:
  0.0 192.5 jit_solution(3850129601855439194)
XLA Ops:
  6.5 0.8 fusion.10
  7.4 1.1 reduce_sum.18
  8.5 1.2 multiply_reduce_fusion
  9.7 1.1 multiply_add_fusion.1
  10.8 10.2 %all_to_all.38 = f32[8,4,2048]{2,0,1:T(8,128)} all-to-all(f32[8,4,2048]{2,0,1:T(8,128)S(1)} %bitcast.15), channel_id=1, replica_groups=mesh['groups'=2,'row'=4,'col'=4] {'row'}, dimensions={1} | all-to-all | bytes 524288 | tf_op jit(solution)/shard_map/all_to_all | solution.py:23
  20.9 0.0 all-gather.2.cloned.1.call-update
  21.0 0.0 copy-start.2
  21.0 0.0 reduce-scatter.3.cloned.1.call-start
  21.0 28.7 %all-gather.2.cloned.1.call-done = f32[128,2048]{1,0:T(8,128)} async-done(((f32[32,2048]{1,0:T(8,128)}), f32[128,2048]{1,0:T(8,128)}) %all-gather.2.cloned.1.call-update) | async-done | bytes 1048592 | tf_op jit(solution)/shard_map/all_gather | solution.py:25
  49.8 17.7 %fusion.11 = f32[128,4096]{1,0:T(8,128)} fusion(f32[128,2048]{1,0:T(8,128)} %all-gather.2.cloned.1.call-done, f32[2048,4096]{1,0:T(8,128)} %param.8), kind=kOutput, calls=%fused_computation.26 | convolution fusion | flops 6442450944 | bytes 36700160 | tf_op jit(solution)/shard_map/dot_general | solution.py:24
  67.4 0.0 reduce-scatter.3.cloned.1.call-update
  67.5 0.0 reduce-scatter.5.cloned.1.call-start
  67.5 31.0 %reduce-scatter.3.cloned.1.call-done = f32[32,4096]{1,0:T(8,128)} async-done(((f32[128,4096]{1,0:T(8,128)}), f32[32,4096]{1,0:T(8,128)}) %reduce-scatter.3.cloned.1.call-update) | async-done | bytes 524304 | tf_op jit(solution)/shard_map/reduce_scatter | solution.py:30
  98.5 1.3 fusion.8
  99.8 0.1 collective-permute-start
  99.9 8.6 %collective-permute-done = f32[32,4096]{1,0:T(8,128)S(1)} collective-permute-done((f32[32,4096]{1,0:T(8,128)S(1)}, f32[32,4096]{1,0:T(8,128)S(1)}, u32[]{:S(2)}, u32[]{:S(2)}) %collective-permute-start) | collective-permute-done | bytes 524320 | tf_op jit(solution)/shard_map/ppermute | solution.py:34
  108.5 0.0 collective-permute-start.1
  108.5 8.6 %collective-permute-done.1 = f32[32,4096]{1,0:T(8,128)S(1)} collective-permute-done((f32[32,4096]{1,0:T(8,128)S(1)}, f32[32,4096]{1,0:T(8,128)S(1)}, u32[]{:S(2)}, u32[]{:S(2)}) %collective-permute-start.1) | collective-permute-done | bytes 524320 | tf_op jit(solution)/shard_map/ppermute | solution.py:34
  117.1 8.6 %collective-permute-done.2 = f32[32,4096]{1,0:T(8,128)S(1)} collective-permute-done((f32[32,4096]{1,0:T(8,128)S(1)}, f32[32,4096]{1,0:T(8,128)S(1)}, u32[]{:S(2)}, u32[]{:S(2)}) %collective-permute-start.2) | collective-permute-done | bytes 524320 | tf_op jit(solution)/shard_map/ppermute | solution.py:34
  125.7 0.8 constant_dynamic-update-slice_fusion.7
  126.5 0.8 constant_dynamic-update-slice_fusion.6
  127.4 0.8 constant_dynamic-update-slice_fusion.5
  128.2 1.0 constant_dynamic-update-slice_fusion.4
  129.2 0.8 constant_dynamic-update-slice_fusion.3
  130.0 0.8 constant_dynamic-update-slice_fusion.2
  130.8 0.8 constant_dynamic-update-slice_fusion.1
  131.7 1.0 constant_dynamic-update-slice_fusion
  132.6 15.8 %fusion = f32[128,2048]{1,0:T(8,128)} fusion(f32[4096,2048]{1,0:T(8,128)} %param.10, f32[256,4096]{1,0:T(8,128)} %constant_dynamic-update-slice_fusion, s32[]{:T(128)S(6)} %select_n.17), kind=kOutput, calls=%fused_computation | convolution fusion | flops 6442450944 | bytes 36700164 | tf_op jit(solution)/shard_map/dot_general | solution.py:39
  148.5 0.0 reduce-scatter.5.cloned.1.call-update
  148.5 27.3 %reduce-scatter.5.cloned.1.call-done = f32[32,2048]{1,0:T(8,128)} async-done(((f32[128,2048]{1,0:T(8,128)}), f32[32,2048]{1,0:T(8,128)}) %reduce-scatter.5.cloned.1.call-update) | async-done | bytes 262160 | tf_op jit(solution)/shard_map/reduce_scatter | solution.py:38
  175.8 9.4 %all_to_all.39 = f32[4,8,2048]{2,1,0:T(8,128)S(1)} all-to-all(f32[4,8,2048]{2,1,0:T(8,128)} %bitcast.17), channel_id=1, replica_groups=mesh['groups'=2,'row'=4,'col'=4] {'row'}, dimensions={0} | all-to-all | bytes 524288 | tf_op jit(solution)/shard_map/all_to_all | solution.py:46
  185.2 0.8 multiply_add_fusion
  (11 shorter events, 0.0 us)
Async XLA Ops:
  6.5 43.2 %all-gather.2.cloned.1.call-start = ((), (), s32[]{:S(2)}) async-start(), calls=%async_computation.4 | async-start | bytes 1310720 | tf_op jit(solution)/shard_map/all_gather | solution.py:25
  21.0 77.6 %copy-start.2 = (f32[4096]{0:T(1024)S(1)}, f32[4096]{0:T(1024)}, u32[]{:S(2)}) copy-start(f32[4096]{0:T(1024)} %param.9) | copy-start | bytes 49156
  21.0 77.6 %reduce-scatter.3.cloned.1.call-start = ((), (), s32[]{:S(2)}) async-start(), calls=%async_computation.5 | async-start | bytes 2621440 | tf_op jit(solution)/shard_map/reduce_scatter | solution.py:30
  67.5 108.3 %reduce-scatter.5.cloned.1.call-start = ((), (), s32[]{:S(2)}) async-start(), calls=%async_computation.6 | async-start | bytes 1310720 | tf_op jit(solution)/shard_map/reduce_scatter | solution.py:38
  98.5 29.7 %copy-start = (f32[32,4096]{1,0:T(8,128)S(1)}, f32[32,4096]{1,0:T(8,128)}, u32[]{:S(2)}) copy-start(f32[32,4096]{1,0:T(8,128)} %reduce-scatter.3.cloned.1.call-done) | copy-start | bytes 1572868
  99.8 8.7 %collective-permute-start = (f32[32,4096]{1,0:T(8,128)S(1)}, f32[32,4096]{1,0:T(8,128)S(1)}, u32[]{:S(2)}, u32[]{:S(2)}) collective-permute-start(f32[32,4096]{1,0:T(8,128)S(1)} %fusion.8), channel_id=1, source_target_pairs={{0,4},{4,8},{8,12},{12,0},{1,5},{5,9},{9,13},{13,1},{2,6},{6,10},{... | collective-permute-start | bytes 1572872 | tf_op jit(solution)/shard_map/ppermute | solution.py:34
  108.5 8.6 %collective-permute-start.1 = (f32[32,4096]{1,0:T(8,128)S(1)}, f32[32,4096]{1,0:T(8,128)S(1)}, u32[]{:S(2)}, u32[]{:S(2)}) collective-permute-start(f32[32,4096]{1,0:T(8,128)S(1)} %collective-permute-done), channel_id=1, source_target_pairs={{0,4},{4,8},{8,12},{12,0},{1,5},{5,9},{9,13},{13,1},{2,6},{6,10},{... | collective-permute-start | bytes 1572872 | tf_op jit(solution)/shard_map/ppermute | solution.py:34
  117.1 8.6 %collective-permute-start.2 = (f32[32,4096]{1,0:T(8,128)S(1)}, f32[32,4096]{1,0:T(8,128)S(1)}, u32[]{:S(2)}, u32[]{:S(2)}) collective-permute-start(f32[32,4096]{1,0:T(8,128)S(1)} %collective-permute-done.1), channel_id=1, source_target_pairs={{0,4},{4,8},{8,12},{12,0},{1,5},{5,9},{9,13},{13,1},{2,6},{6,10},{... | collective-permute-start | bytes 1572872 | tf_op jit(solution)/shard_map/ppermute | solution.py:34
  132.6 52.6 %copy-start.1 = (f32[8,8192]{1,0:T(8,128)S(1)}, f32[8,8192]{1,0:T(8,128)}, u32[]{:S(2)}) copy-start(f32[8,8192]{1,0:T(8,128)} %param.6) | copy-start | bytes 786436
  132.6 52.6 %copy-start.3 = (f32[8192]{0:T(1024)S(1)}, f32[8192]{0:T(1024)}, u32[]{:S(2)}) copy-start(f32[8192]{0:T(1024)} %param.11) | copy-start | bytes 98308
Sparse Core Ops, SparseCore 0:
  21.1 28.6 all-gather.1
  67.6 30.9 reduce-scatter.2
  148.6 27.1 reduce-scatter.4
